TPU v7x, 256 devices: a whole 4x4x8 slice. The times are simulated.
256 devices in a mesh: batch: 8 (over x, core), tensor: 32 (over y, z).
Axes of the slice: x: 4, y: 4, z: 8, core: 2. Of those that a mesh axis runs over, the one named last changes fastest.
Arguments:
- inputs: bfloat16 [4, 8, 32, 4096], P(None, 'batch', 'tensor'), may hold values from -6 to 6
- norm_gain: float32 [4096], replicated, may hold values from 0.5 to 1.5
- norm_bias: float32 [4096], replicated, may hold values from -3 to 3
- qkv_weight: bfloat16 [4096, 3, 4096], P(None, None, 'tensor'), may hold values from -0.09375 to 0.09375
- out_weight: bfloat16 [4096, 4096], P('tensor'), may hold values from -0.375 to 0.375
- in_weight: bfloat16 [4096, 8192], P(None, 'tensor'), may hold values from -0.09375 to 0.09375
- in_bias: float32 [8192], P('tensor'), may hold values from -3 to 3
- down_weight: bfloat16 [8192, 4096], P('tensor'), may hold values from -0.0625 to 0.0625
- down_bias: float32 [4096], replicated, may hold values from -3 to 3
- page_pool: bfloat16 [128, 2, 128, 4096], P('batch', None, None, 'tensor'), may hold values from -103 to 103
- old_cache: bfloat16 [8, 32, 2, 64, 4096], P('batch', None, None, None, 'tensor'), may hold values from -103 to 103, as said below
- page_table: int32 [32, 4], replicated, may hold values from 0 to 127, as said below
- prompt_length: int32 [32], replicated, may hold values from 1 to 512, 8192 in all
- parents: int32 [4, 8, 32], replicated, may hold values from 0 to 7
Outputs:
- outputs: float32 [4, 8, 32, 4096], P(None, 'batch', 'tensor')
Inputs may be any that keep to these rules, and one draw needn't show every extreme that they name: `old_cache`: key and value entries of the beams' generated tokens. `page_table`: every pool page is named exactly once in the table. The pool is cut into as many equal blocks of consecutive pages as the batch axis has devices; request r names only pages of block r modulo that count.
All inputs are finite; a program needn't handle non-finite values.
Results may differ from a plain program's by a relative error of at most 0.034.
Values may be sent and summed in bfloat16 or wider, within the bound.
No kernel may reach another device: no remote copies, remote signals or barrier semaphores. Data moves between devices by JAX's collectives and lax.ppermute only.
A program may use at most 128 MiB of HBM per device.

v0:
```python
import math
import jax
import jax.numpy as jnp
from jax import lax
from jax.sharding import PartitionSpec as P

HDIM = 256
ROT = 64
BEAMS = 8
NEG_FILL = -1e30


def partner(value, axis, bit):
    return lax.ppermute(value, axis, [(i, i ^ 1 << bit) for i in range(lax.axis_size(axis))])


def normalize(row_block, norm_gain, norm_bias):
    widened = row_block.astype(jnp.float32)
    center = jnp.mean(widened, axis=-1, keepdims=True)
    shifted = widened - center
    variance = jnp.mean(shifted * shifted, axis=-1, keepdims=True)
    return shifted * lax.rsqrt(variance + 1e-05) * norm_gain + norm_bias


def rotate_local(vectors, position, first_column):
    half_count = vectors.shape[-1] // 2
    doubled = (first_column + 2 * jnp.arange(half_count)) % HDIM
    exponent = doubled.astype(jnp.float32) / ROT
    frequency = jnp.where(doubled < ROT, jnp.exp(-exponent * math.log(10000.0)), 0.0)
    angles = position[..., None] * frequency
    cosine = jnp.cos(angles)
    sine_part = jnp.sin(angles)
    halves = vectors.reshape(vectors.shape[:-1] + (half_count, 2))
    even_part = halves[..., 0]
    odd_part = halves[..., 1]
    turned = jnp.stack(
        [even_part * cosine - odd_part * sine_part, odd_part * cosine + even_part * sine_part],
        axis=-1,
    )
    return turned.reshape(vectors.shape)


def on_device(
    inputs,
    norm_gain,
    norm_bias,
    qkv_weight,
    out_weight,
    in_weight,
    in_bias,
    down_weight,
    down_bias,
    page_pool,
    old_cache,
    page_table,
    prompt_length,
    parents,
):
    batch_index = lax.axis_index("batch")
    tensor_index = lax.axis_index("tensor")
    groups = lax.axis_size("batch")
    steps = inputs.shape[0]
    model_width = inputs.shape[3]
    columns = qkv_weight.shape[2]
    requests = page_table.shape[0]
    history = old_cache.shape[3]
    page_count = page_table.shape[1]
    page_size = page_pool.shape[2]
    pool_dev = page_pool.shape[0]
    prompt_span = page_count * page_size
    local_reqs = requests // groups
    scale_factor = HDIM ** (-0.5)
    first_column = tensor_index * columns
    normed = normalize(inputs[:, 0], norm_gain, norm_bias).astype(jnp.bfloat16)
    rows = lax.all_gather(normed, "tensor", axis=1, tiled=True)
    flat = rows.reshape(steps * requests, model_width)
    qkv_flat = qkv_weight.reshape(model_width, 3 * columns)
    projected = jnp.dot(flat, qkv_flat, preferred_element_type=jnp.float32).reshape(
        steps, requests, 3 * columns
    )
    ffn = jnp.dot(flat, in_weight, preferred_element_type=jnp.float32).reshape(steps, requests, -1)
    hidden = jax.nn.gelu(ffn + in_bias, approximate=True).astype(jnp.bfloat16)
    position = (
        prompt_length[None, :] + history + jnp.arange(steps, dtype=jnp.int32)[:, None]
    ).astype(jnp.float32)
    queries = rotate_local(projected[..., :columns], position, first_column).astype(jnp.bfloat16)
    fresh_keys = rotate_local(projected[..., columns : 2 * columns], position, first_column).astype(
        jnp.bfloat16
    )
    fresh_values = projected[..., 2 * columns :].astype(jnp.bfloat16)
    query_all = lax.all_gather(queries[:, None], "batch", axis=1, tiled=True)
    beam_ids = jnp.broadcast_to(jnp.arange(BEAMS, dtype=jnp.int32)[:, None], (BEAMS, requests))
    new_ok_steps = []
    old_ok_steps = []
    for step_index in range(steps):
        lineage = beam_ids
        per_t = [None] * steps
        for back_step in range(step_index, -1, -1):
            per_t[back_step] = lineage == batch_index
            lineage = jnp.take_along_axis(parents[back_step], lineage, axis=0)
        for t in range(step_index + 1, steps):
            per_t[t] = jnp.zeros((BEAMS, requests), bool)
        new_ok_steps.append(jnp.stack(per_t, axis=-1))
        old_ok_steps.append(lineage == batch_index)
    new_ok = jnp.stack(new_ok_steps, axis=0)
    old_ok = jnp.stack(old_ok_steps, axis=0)
    old_keys = old_cache[0, :, 0]
    old_values = old_cache[0, :, 1]
    old_scores = jnp.einsum(
        "sbrc,rhc->sbrh", query_all, old_keys, preferred_element_type=jnp.float32
    )
    new_scores = jnp.einsum(
        "sbrc,trc->sbrt", query_all, fresh_keys, preferred_element_type=jnp.float32
    )
    query_local = lax.dynamic_index_in_dim(
        query_all.reshape(steps, BEAMS, local_reqs, groups, columns), batch_index, 3, False
    )
    table_local = (
        lax.dynamic_index_in_dim(
            page_table.reshape(local_reqs, groups, page_count), batch_index, 1, False
        )
        - batch_index * pool_dev
    )
    table_local = jnp.clip(table_local, 0, pool_dev - 1)
    length_local = lax.dynamic_index_in_dim(
        prompt_length.reshape(local_reqs, groups), batch_index, 1, False
    )
    pages = page_pool[table_local]
    prompt_keys = pages[:, :, 0].reshape(local_reqs, prompt_span, columns)
    prompt_values = pages[:, :, 1].reshape(local_reqs, prompt_span, columns)
    prompt_scores = jnp.einsum(
        "sbrc,rtc->sbrt", query_local, prompt_keys, preferred_element_type=jnp.float32
    )
    other = partner((old_scores, new_scores, prompt_scores), "tensor", 0)
    old_scores = (old_scores + other[0]) * scale_factor
    new_scores = (new_scores + other[1]) * scale_factor
    prompt_scores = (prompt_scores + other[2]) * scale_factor
    old_mask = old_ok[..., None]
    old_masked = jnp.where(old_mask, old_scores, NEG_FILL)
    new_masked = jnp.where(new_ok, new_scores, NEG_FILL)
    chain_peak = jnp.maximum(jnp.max(old_masked, axis=-1), jnp.max(new_masked, axis=-1))
    old_w = jnp.where(old_mask, jnp.exp(old_masked - chain_peak[..., None]), 0.0)
    new_w = jnp.where(new_ok, jnp.exp(new_masked - chain_peak[..., None]), 0.0)
    chain_total = jnp.sum(old_w, axis=-1) + jnp.sum(new_w, axis=-1)
    chain_mix = jnp.einsum(
        "sbrh,rhc->sbrc", old_w.astype(jnp.bfloat16), old_values, preferred_element_type=jnp.float32
    ) + jnp.einsum(
        "sbrt,trc->sbrc",
        new_w.astype(jnp.bfloat16),
        fresh_values,
        preferred_element_type=jnp.float32,
    )
    prompt_mask = (jnp.arange(prompt_span)[None, :] < length_local[:, None])[None, None]
    prompt_masked = jnp.where(prompt_mask, prompt_scores, NEG_FILL)
    prompt_peak = jnp.max(prompt_masked, axis=-1)
    prompt_w = jnp.where(prompt_mask, jnp.exp(prompt_masked - prompt_peak[..., None]), 0.0)
    prompt_total = jnp.sum(prompt_w, axis=-1)
    prompt_mix = jnp.einsum(
        "sbrt,rtc->sbrc",
        prompt_w.astype(jnp.bfloat16),
        prompt_values,
        preferred_element_type=jnp.float32,
    )
    slot_hit = (jnp.arange(groups) == batch_index)[None, None, None, :]

    def spread(values, fill):
        placed = jnp.where(slot_hit, values[..., None], fill)
        return placed.reshape(values.shape[:2] + (requests,))

    def spread_mix(values):
        placed = jnp.where(slot_hit[..., None], values[:, :, :, None, :], 0.0)
        return placed.reshape(values.shape[:2] + (requests, columns))

    p_peak = spread(prompt_peak, NEG_FILL)
    p_total = spread(prompt_total, 0.0)
    p_mix = spread_mix(prompt_mix)
    peak = jnp.maximum(chain_peak, p_peak)
    f_chain = jnp.exp(chain_peak - peak)
    f_prompt = jnp.exp(p_peak - peak)
    total = chain_total * f_chain + p_total * f_prompt
    mix = chain_mix * f_chain[..., None] + p_mix * f_prompt[..., None]
    packed = jnp.concatenate([mix, peak[..., None], total[..., None]], axis=-1)
    received = lax.all_to_all(packed, "batch", 1, 1, tiled=True)
    r_mix = received[..., :columns]
    r_peak = received[..., columns]
    r_total = received[..., columns + 1]
    g_peak = jnp.max(r_peak, axis=1, keepdims=True)
    factor = jnp.exp(r_peak - g_peak)
    all_total = jnp.sum(r_total * factor, axis=1)
    all_mix = jnp.sum(r_mix * factor[..., None], axis=1)
    attention = (all_mix / all_total[..., None]).astype(jnp.bfloat16)
    update = jnp.einsum(
        "src,cd->rsd", attention, out_weight, preferred_element_type=jnp.float32
    ) + jnp.einsum("srf,fd->rsd", hidden, down_weight, preferred_element_type=jnp.float32)
    summed = lax.psum_scatter(update, "tensor", scatter_dimension=0, tiled=True)
    result = inputs[:, 0].astype(jnp.float32) + jnp.transpose(summed, (1, 0, 2)) + down_bias
    return result[:, None]


def solution(mesh):
    in_specs = (
        P(None, "batch", "tensor", None),
        P(),
        P(),
        P(None, None, "tensor"),
        P("tensor", None),
        P(None, "tensor"),
        P("tensor"),
        P("tensor", None),
        P(),
        P("batch", None, None, "tensor"),
        P("batch", None, None, None, "tensor"),
        P(),
        P(),
        P(),
    )
    out_specs = P(None, "batch", "tensor", None)
    return jax.shard_map(
        on_device, mesh=mesh, in_specs=in_specs, out_specs=out_specs, check_vma=False
    )
```

profile of v0, /device:TPU:2, one launch (start us, length us, event | category | flops | bytes accessed | tf_op | source)
XLA Modules:
  0.0 358.6 jit_solution(18365220035608578066)
XLA Ops:
  6.5 1.1 convert_reduce_fusion
  7.6 1.0 fusion.82
  8.6 1.5 fusion.85
  10.2 0.7 slice_bitcast_fusion
  11.0 1.4 gather_fusion.7
  12.6 1.4 gather_fusion.4
  14.0 1.4 gather_fusion.8
  15.7 1.4 gather_fusion.2
  17.1 1.4 gather_fusion.9
  18.7 1.4 gather_fusion.1
  20.1 1.4 gather_fusion.10
  21.9 1.4 gather_fusion.5
  23.5 1.4 gather_fusion.6
  25.2 1.4 gather_fusion.3
  27.2 4.7 %copy.447 = bf16[4096,3,128]{0,2,1:T(8,128)(2,1)} copy(bf16[4096,3,128]{2,0,1:T(8,128)(2,1)} %param.19) | data formatting | bytes 6291456 | tf_op args[3]
  32.9 2.0 gather_fusion
  35.0 1.1 fusion.126
  36.0 53.7 %all-gather.2.cloned.1.call-done = bf16[4,32,4096]{2,0,1:T(4,128)(2,1)} async-done(((bf16[4,1,4096]{2,0,1:T(4,128)(2,1)}), bf16[4,32,4096]{2,0,1:T(4,128)(2,1)}) %all-gather.2.cloned.1.call-update) | async-done | bytes 1048592 | tf_op jit(solution)/shard_map/all_gather | solution.py:75
  89.7 3.4 fusion.13
  93.1 0.6 fusion.92
  95.4 12.8 %all_gather.7 = bf16[4,8,32,128]{3,2,0,1:T(8,128)(2,1)S(1)} all-gather(bf16[4,1,32,128]{3,2,0,1:T(8,128)(2,1)S(1)} %copy.454), channel_id=1, replica_groups=mesh['batch'=8,'tensor'=32] {'batch'}, dimensions={1}, use_global_device_ids=true | all-gather | bytes 294912 | tf_op jit(solution)/shard_map/all_gather | solution.py:91
  108.5 1.3 convolution_bitcast_fusion.4
  109.7 0.6 collective-permute-start.1
  110.3 1.4 convolution_bitcast_fusion.2
  111.8 1.5 collective-permute-start
  113.4 1.3 convolution_bitcast_fusion.3
  114.7 0.8 collective-permute-start.2
  115.5 3.4 collective-permute-done.1
  118.9 0.7 copy-done.5
  119.9 10.2 %collective-permute-done = f32[4,8,32,64]{3,1,0,2:T(8,128)S(1)} collective-permute-done((f32[4,8,32,64]{3,1,0,2:T(8,128)S(1)}, f32[4,8,32,64]{3,1,0,2:T(8,128)S(1)}, u32[]{:S(2)}, u32[]{:S(2)}) %collective-permute-start) | collective-permute-done | bytes 262176 | tf_op jit(solution)/shard_map/ppermute | solution.py:14
  130.6 4.6 %collective-permute-done.2 = f32[4,8,4,512]{3,1,0,2:T(8,128)S(1)} collective-permute-done((f32[4,8,4,512]{3,1,0,2:T(8,128)S(1)}, f32[4,8,4,512]{3,1,0,2:T(8,128)S(1)}, u32[]{:S(2)}, u32[]{:S(2)}) %collective-permute-start.2) | collective-permute-done | bytes 262176 | tf_op jit(solution)/shard_map/ppermute | solution.py:14
  135.3 0.7 fusion.69
  136.0 0.7 fusion.70
  136.8 0.7 copy.473
  137.5 0.7 copy.470
  138.2 1.3 fusion.31
  139.5 1.6 fusion.21
  141.0 0.6 add_bitcast_fusion
  141.7 1.5 copy.478
  143.2 0.8 fusion.29
  144.0 1.4 copy.479
  145.4 1.4 broadcast_in_dim.189
  146.8 1.5 broadcast_in_dim.190
  148.3 1.4 broadcast_in_dim.178
  149.8 1.5 broadcast_in_dim.187
  151.3 1.4 bitcast_maximum_fusion
  152.7 2.0 copy.481
  154.7 2.0 copy.482
  156.6 1.3 convolution_bitcast_fusion.5
  158.0 1.1 fusion.18
  159.1 1.7 convolution_bitcast_fusion.1
  161.3 0.5 copy-done.2
  162.6 18.9 %all_to_all.5 = f32[4,8,32,130]{3,0,2,1:T(4,128)S(1)} all-to-all(f32[4,8,32,130]{3,0,2,1:T(4,128)S(1)} %copy.483), channel_id=1, replica_groups=mesh['batch'=8,'tensor'=32] {'batch'}, dimensions={1} | all-to-all | bytes 1064960 | tf_op jit(solution)/shard_map/all_to_all | solution.py:183
  181.5 1.4 fusion.125
  182.9 1.3 copy.516
  184.2 1.3 copy.517
  186.4 3.0 fusion.10
  189.4 5.0 %fusion = f32[32,4,4096]{2,0,1:T(8,128)} fusion(f32[4,32,4096]{2,1,0:T(8,128)} %fusion.10, bf16[256,4096]{1,0:T(8,128)(2,1)S(1)} %copy-done, bf16[4096,256]{1,0:T(8,128)(2,1)} %param.21, bf16[4,32,4096]{2,0,1:T(4,128)(2,1)S(1)} %copy-done.1, f32[256]{0:T(256)S(1)} %copy-done.13), kind=kOutput, calls=%fused_computation.12 | convolution fusion | flops 537722880 | bytes 9438208 | tf_op jit(solution)/shard_map/srf,fd->rsd/dot_general | solution.py:194
  194.4 4.3 %copy.491 = f32[32,4,4096]{2,1,0:T(4,128)} copy(f32[32,4,4096]{2,0,1:T(8,128)} %fusion) | data formatting | bytes 4194304 | tf_op jit(solution)/shard_map/add | solution.py:192
  198.7 0.6 copy-done.15
  199.3 0.6 dynamic-slice
  199.9 149.7 %all-reduce.3.cloned.1.call-done = f32[32,4,4096]{2,1,0:T(4,128)} async-done(((f32[32,4,4096]{2,1,0:T(4,128)}), f32[32,4,4096]{2,1,0:T(4,128)}) %all-reduce.3.cloned.1.call-update) | async-done | bytes 2097168
  349.6 1.5 fusion.86
  351.1 0.7 copy.492
  (115 shorter events, 7.9 us)
Async XLA Ops:
  6.5 182.9 %copy-start = (bf16[256,4096]{1,0:T(8,128)(2,1)S(1)}, bf16[256,4096]{1,0:T(8,128)(2,1)}, u32[]{:S(2)}) copy-start(bf16[256,4096]{1,0:T(8,128)(2,1)} %param.23) | copy-start | bytes 6291460
  6.5 83.1 %all-gather.2.cloned.1.call-start = ((), (), s32[]{:S(2)}) async-start(), calls=%async_computation.1 | async-start | bytes 1081344 | tf_op jit(solution)/shard_map/all_gather | solution.py:75
  10.1 339.5 %all-reduce.3.cloned.1.call-start = ((), (), s32[]{:S(2)}) async-start(), calls=%async_computation.2 | async-start | bytes 4194304
  27.2 4.9 %copy-start.12 = (s32[32,4]{0,1:T(4,128)S(1)}, s32[32,4]{0,1:T(4,128)}, u32[]{:S(2)}) copy-start(s32[32,4]{0,1:T(4,128)} %param.27) | copy-start | bytes 1540
  27.2 5.2 %copy-start.14 = (s32[32]{0:T(128)S(1)}, s32[32]{0:T(128)}, u32[]{:S(2)}) copy-start(s32[32]{0:T(128)} %param.28) | copy-start | bytes 388
  32.1 98.1 %copy-start.8 = (pred[4,8,32]{1,0,2:T(4,128)(4,1)}, pred[4,8,32]{1,0,2:T(4,128)(4,1)S(1)}, u32[]{:S(2)}) copy-start(pred[4,8,32]{1,0,2:T(4,128)(4,1)S(1)} %copy.446) | copy-start | bytes 3076
  109.7 9.2 %collective-permute-start.1 = (f32[4,8,32,4]{1,3,0,2:T(4,128)S(1)}, f32[4,8,32,4]{1,3,0,2:T(4,128)S(1)}, u32[]{:S(2)}, u32[]{:S(2)}) collective-permute-start(f32[4,8,32,4]{1,3,0,2:T(4,128)S(1)} %convolution_bitcast_fusion.4), channel_id=1, source_target_pairs={{0,1},{1,0},{2,3},{3,2},{4,5},{5,4},{6,7},{7,6},{8,9},{9,8},{10,11... | collective-permute-start | bytes 49160 | tf_op jit(solution)/shard_map/ppermute | solution.py:14
  111.8 18.4 %collective-permute-start = (f32[4,8,32,64]{3,1,0,2:T(8,128)S(1)}, f32[4,8,32,64]{3,1,0,2:T(8,128)S(1)}, u32[]{:S(2)}, u32[]{:S(2)}) collective-permute-start(f32[4,8,32,64]{3,1,0,2:T(8,128)S(1)} %convolution_bitcast_fusion.2), channel_id=1, source_target_pairs={{0,1},{1,0},{2,3},{3,2},{4,5},{5,4},{6,7},{7,6},{8,9},{9,8},{10,11... | collective-permute-start | bytes 786440 | tf_op jit(solution)/shard_map/ppermute | solution.py:14
  114.7 20.5 %collective-permute-start.2 = (f32[4,8,4,512]{3,1,0,2:T(8,128)S(1)}, f32[4,8,4,512]{3,1,0,2:T(8,128)S(1)}, u32[]{:S(2)}, u32[]{:S(2)}) collective-permute-start(f32[4,8,4,512]{3,1,0,2:T(8,128)S(1)} %convolution_bitcast_fusion.3), channel_id=1, source_target_pairs={{0,1},{1,0},{2,3},{3,2},{4,5},{5,4},{6,7},{7,6},{8,9},{9,8},{10,11... | collective-permute-start | bytes 786440 | tf_op jit(solution)/shard_map/ppermute | solution.py:14
  118.9 0.7 copy-start.5
  130.2 5.0 %copy-start.4 = (f32[4,8,32,64]{3,1,0,2:T(8,128)}, f32[4,8,32,64]{3,1,0,2:T(8,128)S(1)}, u32[]{:S(2)}) copy-start(f32[4,8,32,64]{3,1,0,2:T(8,128)S(1)} %collective-permute-done) | copy-start | bytes 786436
  159.0 1.8 copy-start.6
  159.0 1.8 copy-start.9
  159.1 1.8 copy-start.10
  160.8 1.0 copy-start.2
  160.8 1.2 copy-start.3
  185.6 3.8 %copy-start.13 = (f32[256]{0:T(256)S(1)}, f32[256]{0:T(256)}, u32[]{:S(2)}) copy-start(f32[256]{0:T(256)} %param.22) | copy-start | bytes 3076
  186.2 3.2 copy-start.1
  198.7 0.7 copy-start.15
  198.7 150.9 %copy-start.7 = (bf16[4,1,1,4096]{3,0,2,1:T(4,128)(2,1)S(1)}, bf16[4,1,1,4096]{3,0,2,1:T(4,128)(2,1)}, u32[]{:S(2)}) copy-start(bf16[4,1,1,4096]{3,0,2,1:T(4,128)(2,1)} %param.16) | copy-start | bytes 98308
  198.7 150.9 %copy-start.11 = (f32[4096]{0:T(1024)S(1)}, f32[4096]{0:T(1024)}, u32[]{:S(2)}) copy-start(f32[4096]{0:T(1024)} %param.24) | copy-start | bytes 49156
Sparse Core Ops, SparseCore 0:
  10.2 79.4 all-gather.1
  198.8 150.7 all-reduce.2
where the time goes:
time: 360 us; the launch traced here: 359 us
  waiting for transfers between devices  222 us (62%)
  local copies, waits for them, and re-layouts  52.6 us (15%)
  blocking collectives  31.7 us (9%)
  matrix products  18.8 us (5%)
  other arithmetic  17 us (5%)
  between operations  13.9 us (4%)
    unnamed x3, waiting for transfers between devices  150 us
    all_gather x1, waiting for transfers between devices, on_device(): rows = lax.all_gather(normed, 'tensor', axis=1, tiled=True)  53.7 us
    all_to_all x1, blocking collectives, on_device(): received = lax.all_to_all(packed, 'batch', 1, 1, tiled=True)  18.9 us
    ppermute x3, waiting for transfers between devices, partner(): lax.ppermute(value, axis, [(i, i ^ 1 << bit) for i in range(lax.axis_size...  18.2 us
    gather x27, local copies, waits for them, and re-layouts, on_device(): lineage = jnp.take_along_axis(parents[back_step], lineage, axis=0)  15.6 us
    all_gather x1, blocking collectives, on_device(): query_all = lax.all_gather(queries[:, None], 'batch', axis=1, tiled=True)  12.8 us
    unnamed x42, local copies, waits for them, and re-layouts  10.5 us
  transfers between devices with their start and end apart: 5, of which 5 were waited for; matrix products, arithmetic and copies ran while one was open for 8% of the time, Pallas kernels for 0%

commit v1 on v0

--- a/solution.py
+++ b/solution.py
@@ -72,7 +72,9 @@
     scale_factor = HDIM ** (-0.5)
     first_column = tensor_index * columns
     normed = normalize(inputs[:, 0], norm_gain, norm_bias).astype(jnp.bfloat16)
-    rows = lax.all_gather(normed, "tensor", axis=1, tiled=True)
+    rows = jnp.concatenate(
+        lax.all_to_all(jnp.stack([normed] * lax.axis_size("tensor")), "tensor", 0, 0), axis=1
+    )
     flat = rows.reshape(steps * requests, model_width)
     qkv_flat = qkv_weight.reshape(model_width, 3 * columns)
     projected = jnp.dot(flat, qkv_flat, preferred_element_type=jnp.float32).reshape(

time: 360 us -> 341 us (0.947)
  waiting for transfers between devices: 222 us -> 172 us
  local copies, waits for them, and re-layouts: 52.6 us -> 66.6 us
  starting transfers between devices: 3.01 us -> 15.8 us
  other arithmetic: 17 us -> 21.2 us
    all_gather x1 -> x0, waiting for transfers between devices: 53.7 us -> none  [on_device(): rows = lax.all_gather(normed, 'tensor', axis=1, tiled=True)]
    all_to_all x0 -> x1, starting transfers between devices: none -> 11.5 us  [on_device(): lax.all_to_all(jnp.stack([normed] * lax.axis_size('tensor')), 'tensor', 0...]
    unnamed x42 -> x62, local copies, waits for them, and re-layouts: 10.5 us -> 16.1 us
    unnamed x3 -> x2, waiting for transfers between devices: 150 us -> 154 us
  transfers between devices with their start and end apart: 5 -> 5, of which waited for: 5 -> 4; matrix products, arithmetic and copies ran while one was open for 8% -> 10% of each run, Pallas kernels for 0% -> 0%
where the time goes in v1:
time: 341 us; the launch traced here: 339 us
  waiting for transfers between devices  172 us (50%)
  local copies, waits for them, and re-layouts  66.6 us (20%)
  blocking collectives  32 us (9%)
  other arithmetic  21.2 us (6%)
  matrix products  17.7 us (5%)
  starting transfers between devices  15.8 us (5%)
  between operations  13.9 us (4%)
    unnamed x2, waiting for transfers between devices  154 us
    all_to_all x1, blocking collectives, on_device(): received = lax.all_to_all(packed, 'batch', 1, 1, tiled=True)  18.9 us
    ppermute x3, waiting for transfers between devices, partner(): lax.ppermute(value, axis, [(i, i ^ 1 << bit) for i in range(lax.axis_size...  18.4 us
    unnamed x62, local copies, waits for them, and re-layouts  16.1 us
    gather x27, local copies, waits for them, and re-layouts, on_device(): lineage = jnp.take_along_axis(parents[back_step], lineage, axis=0)  15.6 us
    all_gather x1, blocking collectives, on_device(): query_all = lax.all_gather(queries[:, None], 'batch', axis=1, tiled=True)  13.1 us
    all_to_all x1, starting transfers between devices, on_device(): lax.all_to_all(jnp.stack([normed] * lax.axis_size('tensor')), 'tensor', 0...  11.5 us
  transfers between devices with their start and end apart: 5, of which 4 were waited for; matrix products, arithmetic and copies ran while one was open for 10% of the time, Pallas kernels for 0%

profile of v1, /device:TPU:2, one launch (start us, length us, event | category | flops | bytes accessed | tf_op | source)
XLA Modules:
  0.0 339.1 jit_solution(14016843338539248133)
XLA Ops:
  6.5 1.1 convert_reduce_fusion
  7.6 1.0 fusion.83
  8.6 0.9 fusion.89
  9.5 1.5 stack.55
  10.9 11.5 %all-to-all-start = ((bf16[32,4,1,4096]{3,1,2,0:T(4,128)(2,1)}), bf16[32,4,1,4096]{3,1,2,0:T(4,128)(2,1)S(1)}, u32[]{:S(2)}, u32[]{:S(2)}) async-start(bf16[32,4,1,4096]{3,1,2,0:T(4,128)(2,1)} %stack.55), calls=%async_computation | async-start | bytes 2097152 | tf_op jit(solution)/shard_map/all_to_all | solution.py:76
  22.6 1.4 gather_fusion.7
  24.2 1.4 gather_fusion.4
  25.7 1.4 gather_fusion.8
  27.3 1.4 gather_fusion.2
  28.7 1.4 gather_fusion.9
  30.3 1.4 gather_fusion.1
  31.8 1.4 gather_fusion.10
  33.5 1.4 gather_fusion.5
  35.1 1.4 gather_fusion.6
  36.8 1.4 gather_fusion.3
  38.9 4.7 %copy.446 = bf16[4096,3,128]{0,2,1:T(8,128)(2,1)} copy(bf16[4096,3,128]{2,0,1:T(8,128)(2,1)} %param.19) | data formatting | bytes 6291456 | tf_op args[3]
  45.0 2.9 gather_fusion
  49.8 2.3 fusion.129
  52.1 3.0 fusion.11
  56.5 0.9 fusion.131
  57.4 1.0 copy.503
  58.4 1.6 copy.504
  60.0 1.0 copy.455
  61.0 0.9 fusion.130
  61.9 1.0 copy.506
  62.9 1.0 copy.507
  63.9 1.2 fusion.78
  65.9 13.1 %all_gather.3 = bf16[4,8,32,128]{3,2,0,1:T(8,128)(2,1)S(1)} all-gather(bf16[4,1,32,128]{3,2,0,1:T(8,128)(2,1)} %copy.452), channel_id=1, replica_groups=mesh['batch'=8,'tensor'=32] {'batch'}, dimensions={1}, use_global_device_ids=true | all-gather | bytes 294912 | tf_op jit(solution)/shard_map/all_gather | solution.py:93
  79.0 0.8 copy.458
  79.8 1.0 copy.492
  80.8 1.3 convolution_bitcast_fusion.4
  82.1 1.9 collective-permute-start.1
  84.0 1.4 convolution_bitcast_fusion.2
  86.1 2.0 collective-permute-start.2
  88.1 3.2 collective-permute-done.1
  92.1 10.5 %collective-permute-done = f32[4,8,32,64]{3,1,0,2:T(8,128)S(1)} collective-permute-done((f32[4,8,32,64]{3,1,0,2:T(8,128)S(1)}, f32[4,8,32,64]{3,1,0,2:T(8,128)S(1)}, u32[]{:S(2)}, u32[]{:S(2)}) %collective-permute-start) | collective-permute-done | bytes 262176 | tf_op jit(solution)/shard_map/ppermute | solution.py:14
  103.0 4.6 %collective-permute-done.2 = f32[4,8,4,512]{3,1,0,2:T(8,128)S(1)} collective-permute-done((f32[4,8,4,512]{3,1,0,2:T(8,128)S(1)}, f32[4,8,4,512]{3,1,0,2:T(8,128)S(1)}, u32[]{:S(2)}, u32[]{:S(2)}) %collective-permute-start.2) | collective-permute-done | bytes 262176 | tf_op jit(solution)/shard_map/ppermute | solution.py:14
  108.5 0.7 fusion.71
  111.3 1.4 fusion.33
  112.7 1.7 fusion.23
  115.1 1.5 copy.476
  116.6 1.7 fusion.31
  118.4 1.4 copy.477
  119.8 1.4 broadcast_in_dim.189
  121.2 1.5 broadcast_in_dim.190
  122.7 1.4 broadcast_in_dim.178
  124.2 1.5 broadcast_in_dim.187
  125.7 1.4 bitcast_maximum_fusion
  127.1 2.0 copy.479
  129.1 2.0 copy.480
  131.1 1.4 convolution_bitcast_fusion.5
  132.4 1.1 fusion.20
  133.6 1.9 convolution_bitcast_fusion.1
  137.3 18.9 %all_to_all.10 = f32[4,8,32,130]{3,0,2,1:T(4,128)S(1)} all-to-all(f32[4,8,32,130]{3,0,2,1:T(4,128)S(1)} %copy.481), channel_id=1, replica_groups=mesh['batch'=8,'tensor'=32] {'batch'}, dimensions={1} | all-to-all | bytes 1064960 | tf_op jit(solution)/shard_map/all_to_all | solution.py:185
  156.2 1.0 copy-done.1
  157.2 1.4 fusion.128
  158.6 1.3 copy.513
  159.8 1.3 copy.514
  161.5 1.4 fusion.17
  163.0 3.0 fusion.13
  166.0 5.0 %fusion = f32[32,4,4096]{2,0,1:T(8,128)} fusion(f32[4,32,4096]{2,1,0:T(8,128)} %fusion.13, bf16[256,4096]{1,0:T(8,128)(2,1)S(1)} %copy-done, bf16[4096,256]{1,0:T(8,128)(2,1)} %param.21, bf16[32,4,1,4096]{3,1,2,0:T(4,128)(2,1)S(1)} %all-to-all-done, f32[256]{0:T(256)S(1)} %copy-done.23), kind=kOutput, calls=%fused_computation.12 | convolution fusion | flops 537722880 | bytes 9438208 | tf_op jit(solution)/shard_map/srf,fd->rsd/dot_general | solution.py:196
  171.0 4.3 %copy.488 = f32[32,4,4096]{2,1,0:T(4,128)} copy(f32[32,4,4096]{2,0,1:T(8,128)} %fusion) | data formatting | bytes 4194304 | tf_op jit(solution)/shard_map/add | solution.py:194
  176.5 153.5 %all-reduce.3.cloned.1.call-done = f32[32,4,4096]{2,1,0:T(4,128)} async-done(((f32[32,4,4096]{2,1,0:T(4,128)}), f32[32,4,4096]{2,1,0:T(4,128)}) %all-reduce.3.cloned.1.call-update) | async-done | bytes 2097168
  330.1 1.5 fusion.84
  (135 shorter events, 17.1 us)
Async XLA Ops:
  6.5 159.5 %copy-start = (bf16[256,4096]{1,0:T(8,128)(2,1)S(1)}, bf16[256,4096]{1,0:T(8,128)(2,1)}, u32[]{:S(2)}) copy-start(bf16[256,4096]{1,0:T(8,128)(2,1)} %param.23) | copy-start | bytes 6291460
  6.5 16.0 %copy-start.18 = (s32[4,8,32]{2,1,0:T(8,128)S(1)}, s32[4,8,32]{2,1,0:T(8,128)}, u32[]{:S(2)}) copy-start(s32[4,8,32]{2,1,0:T(8,128)} %param.29) | copy-start | bytes 12292
  10.9 41.1 %all-to-all-start = ((bf16[32,4,1,4096]{3,1,2,0:T(4,128)(2,1)}), bf16[32,4,1,4096]{3,1,2,0:T(4,128)(2,1)S(1)}, u32[]{:S(2)}, u32[]{:S(2)}) async-start(bf16[32,4,1,4096]{3,1,2,0:T(4,128)(2,1)} %stack.55), calls=%async_computation | async-start | bytes 2097152 | tf_op jit(solution)/shard_map/all_to_all | solution.py:76
  22.4 307.6 %all-reduce.3.cloned.1.call-start = ((), (), s32[]{:S(2)}) async-start(), calls=%async_computation.2 | async-start | bytes 4194304
  38.8 4.9 %copy-start.22 = (s32[32,4]{0,1:T(4,128)S(1)}, s32[32,4]{0,1:T(4,128)}, u32[]{:S(2)}) copy-start(s32[32,4]{0,1:T(4,128)} %param.27) | copy-start | bytes 1540
  38.9 5.2 %copy-start.24 = (s32[32]{0:T(128)S(1)}, s32[32]{0:T(128)}, u32[]{:S(2)}) copy-start(s32[32]{0:T(128)} %param.28) | copy-start | bytes 388
  43.7 58.9 %copy-start.13 = (pred[4,8,32]{1,0,2:T(4,128)(4,1)}, pred[4,8,32]{1,0,2:T(4,128)(4,1)S(1)}, u32[]{:S(2)}) copy-start(pred[4,8,32]{1,0,2:T(4,128)(4,1)S(1)} %copy.444) | copy-start | bytes 3076
  80.8 5.0 %copy-start.9 = (bf16[4,4,1,128,128]{4,3,2,1,0:T(8,128)(2,1)S(1)}, bf16[4,4,1,128,128]{4,3,2,1,0:T(8,128)(2,1)}, u32[]{:S(2)}) copy-start(bf16[4,4,1,128,128]{4,3,2,1,0:T(8,128)(2,1)} %get-tuple-element.14) | copy-start | bytes 1572868
  82.1 9.3 %copy-start.4 = (f32[4,8,32,4]{1,3,0,2:T(4,128)}, f32[4,8,32,4]{1,3,0,2:T(4,128)S(1)}, u32[]{:S(2)}) copy-start(f32[4,8,32,4]{1,3,0,2:T(4,128)S(1)} %convolution_bitcast_fusion.4) | copy-start | bytes 49156
  82.1 26.3 %copy-start.15 = (pred[4,512]{1,0:T(4,128)(4,1)S(1)}, pred[4,512]{1,0:T(4,128)(4,1)}, u32[]{:S(2)}) copy-start(pred[4,512]{1,0:T(4,128)(4,1)} %iota_compare_fusion) | copy-start | bytes 6148
  82.1 26.4 %copy-start.20 = (pred[32]{0:T(512)(128)(4,1)S(1)}, pred[32]{0:T(512)(128)(4,1)}, u32[]{:S(2)}) copy-start(pred[32]{0:T(512)(128)(4,1)} %broadcast_in_dim.174) | copy-start | bytes 100
  82.1 9.3 %collective-permute-start.1 = (f32[4,8,32,4]{1,3,0,2:T(4,128)S(1)}, f32[4,8,32,4]{1,3,0,2:T(4,128)S(1)}, u32[]{:S(2)}, u32[]{:S(2)}) collective-permute-start(f32[4,8,32,4]{1,3,0,2:T(4,128)S(1)} %convolution_bitcast_fusion.4), channel_id=1, source_target_pairs={{0,1},{1,0},{2,3},{3,2},{4,5},{5,4},{6,7},{7,6},{8,9},{9,8},{10,11... | collective-permute-start | bytes 49160 | tf_op jit(solution)/shard_map/ppermute | solution.py:14
  85.4 17.2 %copy-start.2 = (f32[4,8,32,64]{3,1,0,2:T(8,128)}, f32[4,8,32,64]{3,1,0,2:T(8,128)S(1)}, u32[]{:S(2)}) copy-start(f32[4,8,32,64]{3,1,0,2:T(8,128)S(1)} %convolution_bitcast_fusion.2) | copy-start | bytes 786436
  85.4 17.2 %collective-permute-start = (f32[4,8,32,64]{3,1,0,2:T(8,128)S(1)}, f32[4,8,32,64]{3,1,0,2:T(8,128)S(1)}, u32[]{:S(2)}, u32[]{:S(2)}) collective-permute-start(f32[4,8,32,64]{3,1,0,2:T(8,128)S(1)} %convolution_bitcast_fusion.2), channel_id=1, source_target_pairs={{0,1},{1,0},{2,3},{3,2},{4,5},{5,4},{6,7},{7,6},{8,9},{9,8},{10,11... | collective-permute-start | bytes 786440 | tf_op jit(solution)/shard_map/ppermute | solution.py:14
  86.1 21.6 %collective-permute-start.2 = (f32[4,8,4,512]{3,1,0,2:T(8,128)S(1)}, f32[4,8,4,512]{3,1,0,2:T(8,128)S(1)}, u32[]{:S(2)}, u32[]{:S(2)}) collective-permute-start(f32[4,8,4,512]{3,1,0,2:T(8,128)S(1)} %convolution_bitcast_fusion.3), channel_id=1, source_target_pairs={{0,1},{1,0},{2,3},{3,2},{4,5},{5,4},{6,7},{7,6},{8,9},{9,8},{10,11... | collective-permute-start | bytes 786440 | tf_op jit(solution)/shard_map/ppermute | solution.py:14
  91.4 0.7 copy-start.10
  102.6 5.9 %copy-start.8 = (f32[4,8,32,64]{3,1,0,2:T(8,128)}, f32[4,8,32,64]{3,1,0,2:T(8,128)S(1)}, u32[]{:S(2)}) copy-start(f32[4,8,32,64]{3,1,0,2:T(8,128)S(1)} %collective-permute-done) | copy-start | bytes 786436
  103.0 22.7 %copy-start.21 = (pred[32]{0:T(512)(128)(4,1)S(1)}, pred[32]{0:T(512)(128)(4,1)}, u32[]{:S(2)}) copy-start(pred[32]{0:T(512)(128)(4,1)} %broadcast_in_dim.174) | copy-start | bytes 100
  107.6 0.7 copy-start.3
  111.3 19.7 %copy-start.16 = (pred[4,512]{1,0:T(4,128)(4,1)S(1)}, pred[4,512]{1,0:T(4,128)(4,1)}, u32[]{:S(2)}) copy-start(pred[4,512]{1,0:T(4,128)(4,1)} %iota_compare_fusion) | copy-start | bytes 6148
  133.5 1.9 copy-start.5
  133.5 1.9 copy-start.11
  133.5 1.9 copy-start.14
  133.6 1.9 copy-start.17
  135.5 1.0 copy-start.6
  135.5 1.2 copy-start.7
  156.2 1.0 copy-start.1
  161.3 4.7 %copy-start.23 = (f32[256]{0:T(256)S(1)}, f32[256]{0:T(256)}, u32[]{:S(2)}) copy-start(f32[256]{0:T(256)} %param.22) | copy-start | bytes 3076
  175.3 0.7 copy-start.25
  175.3 154.8 %copy-start.12 = (bf16[4,1,1,4096]{3,0,2,1:T(4,128)(2,1)S(1)}, bf16[4,1,1,4096]{3,0,2,1:T(4,128)(2,1)}, u32[]{:S(2)}) copy-start(bf16[4,1,1,4096]{3,0,2,1:T(4,128)(2,1)} %param.16) | copy-start | bytes 98308
  175.3 154.8 %copy-start.19 = (f32[4096]{0:T(1024)S(1)}, f32[4096]{0:T(1024)}, u32[]{:S(2)}) copy-start(f32[4096]{0:T(1024)} %param.24) | copy-start | bytes 49156
Sparse Core Ops, SparseCore 0:
  175.4 154.6 all-reduce.2
